TPU v7x, 32 devices: a whole 2x2x4 slice. The times are simulated.
32 devices in a mesh: depth: 8 (over z, y), rows: 4 (over x, core).
Axes of the slice: x: 2, y: 2, z: 4, core: 2. Of those that a mesh axis runs over, the one named last changes fastest.
Arguments:
- density_raw: bfloat16 [256, 64, 1024], P('depth', 'rows'), may hold values from -6 to 6
- colour_raw: bfloat16 [3, 256, 64, 1024], P(None, 'depth', 'rows'), may hold values from -6 to 6
- target: float32 [3, 64, 1024], P(None, 'rows'), may hold values from 0 to 1
- slab_rank: int32 [8], replicated, may hold values from 0 to 7, each once
Outputs:
- grad_density: float32 [256, 64, 1024], P('depth', 'rows')
- grad_colour: float32 [3, 256, 64, 1024], P(None, 'depth', 'rows')
Inputs may be any that keep to these rules, and one draw needn't show every extreme that they name: slab_rank is a permutation: every slab has its own position along the rays.
All inputs are finite; a program needn't handle non-finite values.
Results may differ from a plain program's by a relative error of at most 0.0003.
Values may be sent and summed in bfloat16 or wider, within the bound.
No kernel may reach another device: no remote copies, remote signals or barrier semaphores. Data moves between devices by JAX's collectives and lax.ppermute only.
A program may use at most 128 MiB of HBM per device.

v0:
```python
import jax
import jax.numpy as jnp
from jax import lax
from jax.sharding import PartitionSpec as P

optical_depth = 2.5
smooth_weight = 0.05


def extended(value, sides, width):
    for axis, dim in sides:
        peers, length = (lax.axis_size(axis), value.shape[dim])
        up = [(i, (i + 1) % peers) for i in range(peers - 1)]
        down = [(j, i) for i, j in up]
        last = lax.slice_in_dim(value, length - width, length, axis=dim)
        initial = lax.slice_in_dim(value, 0, width, axis=dim)
        before = lax.ppermute(last, axis, up)
        after = lax.ppermute(initial, axis, down)
        value = jnp.concatenate([before, value, after], axis=dim)
    return value


def along_rays(matrix, values):
    shape = values.shape
    flat = values.reshape(shape[0], shape[1], -1)
    mixed = jnp.einsum("ij,cjp->cip", matrix, flat, precision=lax.Precision.HIGHEST)
    return mixed.reshape(shape)


def triangles(count):
    index = jnp.arange(count, dtype=jnp.int32)
    before = (index[None, :] < index[:, None]).astype(jnp.float32)
    after = (index[None, :] > index[:, None]).astype(jnp.float32)
    return (before, after)


def slab_terms(density, colour_raw, step_depth):
    dense = density.astype(jnp.float32)
    colour = jax.nn.sigmoid(colour_raw.astype(jnp.float32))
    depth_term = step_depth * jax.nn.softplus(dense)
    opacity = -jnp.expm1(-depth_term)
    kept = jnp.exp(-depth_term)
    before, after = triangles(dense.shape[0])
    front_light = jnp.exp(-along_rays(before, depth_term[None]))[0]
    through = front_light * kept
    passing = jnp.exp(-jnp.sum(depth_term, axis=0))
    weighted = front_light[None] * opacity[None] * colour
    behind_local = along_rays(after, weighted) / through[None]
    after_light = passing[None] / through
    partial_value = jnp.concatenate([jnp.sum(weighted, axis=1), passing[None]], axis=0)
    return (partial_value, (dense, colour, opacity, behind_local, after_light, front_light))


def slab_gradients(saved, scaled_residual, scaled_behind, slices_total):
    dense, colour, opacity, behind_local, after_light, front_light = saved
    lit = front_light * opacity
    grad_colour = slices_total * scaled_residual[:, None] * lit[None] * colour * (1.0 - colour)
    inner = (
        jnp.sum(scaled_residual[:, None] * (colour - behind_local), axis=0)
        - after_light * scaled_behind[None]
    )
    grad_density = optical_depth * front_light * (1.0 - opacity) * jax.nn.sigmoid(dense) * inner
    return (grad_density, grad_colour)


def composite(partials, slab_rank, target_piece):
    count = partials.shape[1]
    one_hot = (slab_rank[:, None] == jnp.arange(count, dtype=jnp.int32)[None]).astype(
        partials.dtype
    )
    ordered = jnp.einsum("sk,csl->ckl", one_hot, partials, precision=lax.Precision.HIGHEST)
    emitted, kept = (ordered[:3], ordered[3:])
    before, after = triangles(count)
    front = jnp.exp(along_rays(before, jnp.log(kept)))
    weighted = front * emitted
    behind = along_rays(after, weighted) / (front * kept)
    residual = jnp.sum(weighted, axis=1) - target_piece
    scaled_residual = front * residual[:, None]
    scaled_behind = front * jnp.sum(residual[:, None] * behind, axis=0, keepdims=True)
    stacked = jnp.concatenate([scaled_residual, scaled_behind], axis=0)
    return jnp.einsum("sk,ckl->csl", one_hot, stacked, precision=lax.Precision.HIGHEST)


def smooth_rims(density_raw, slices_dev, rows_dev):
    padded = extended(density_raw, (("depth", 0), ("rows", 1)), 1).astype(jnp.float32)
    centre = padded[1:-1, 1:-1]
    slice_index = lax.axis_index("depth") * slices_dev + jnp.arange(slices_dev, dtype=jnp.int32)
    row_index = lax.axis_index("rows") * rows_dev + jnp.arange(rows_dev, dtype=jnp.int32)
    last_slice = slices_dev * lax.axis_size("depth") - 1
    last_row = rows_dev * lax.axis_size("rows") - 1
    below = jnp.where((slice_index > 0)[:, None, None], centre - padded[:-2, 1:-1], 0.0)
    above = jnp.where((slice_index < last_slice)[:, None, None], centre - padded[2:, 1:-1], 0.0)
    upper = jnp.where((row_index > 0)[None, :, None], centre - padded[1:-1, :-2], 0.0)
    lower = jnp.where((row_index < last_row)[None, :, None], centre - padded[1:-1, 2:], 0.0)
    return 2.0 * smooth_weight * (below + above + upper + lower)


def local(density_raw, colour_raw, target, slab_rank):
    slices_dev = density_raw.shape[0]
    rows_dev = density_raw.shape[1]
    width = density_raw.shape[2]
    depth_count = lax.axis_size("depth")
    slices_total = slices_dev * depth_count
    partial_value, saved = slab_terms(density_raw, colour_raw, optical_depth / slices_total)
    pixels = rows_dev * width
    stacked = partial_value.reshape(4, 1, pixels)
    target_flat = target.reshape(3, pixels)
    position = lax.axis_index("depth")
    received = lax.all_gather(stacked, "depth", axis=1, tiled=True)
    answers = composite(received, slab_rank, target_flat)
    mine = lax.dynamic_index_in_dim(answers, position, 1, keepdims=False)
    mine = mine.reshape(4, rows_dev, width)
    grad_density, grad_colour = slab_gradients(saved, mine[:3], mine[3], slices_total)
    grad_density = grad_density + smooth_rims(density_raw, slices_dev, rows_dev)
    return (grad_density, grad_colour)


def solution(mesh):
    placed = (P("depth", "rows", None), P(None, "depth", "rows", None), P(None, "rows", None), P())
    return jax.shard_map(
        local,
        mesh=mesh,
        in_specs=placed,
        out_specs=(P("depth", "rows", None), P(None, "depth", "rows", None)),
        check_vma=False,
    )
```

profile of v0, /device:TPU:0, one launch (start us, length us, event | category | flops | bytes accessed | tf_op | source)
XLA Modules:
  0.0 106.4 jit_solution(17140207208497940315)
XLA Ops:
  7.2 2.4 %fusion.16 = f32[32,16,1024]{2,1,0:T(8,128)S(1)} fusion(bf16[32,16,1024]{2,1,0:T(8,128)(2,1)} %param.4), kind=kLoop, calls=%fused_computation.28 | loop fusion | flops 4194304 | bytes 3145728 | tf_op jit(solution)/shard_map/mul | solution.py:40
  9.7 1.2 %copy.40 = f32[4,8,16,1024]{3,1,2,0:T(8,128)S(1)} copy(f32[4,8,16,1024]{3,2,1,0:T(8,128)S(1)} %bitcast.83) | data formatting | bytes 4194304
  10.9 1.2 %fusion = f32[16384,32]{0,1:T(8,128)S(1)} fusion(f32[32,16384]{1,0:T(8,128)S(1)} %bitcast.81), kind=kOutput, calls=%fused_computation.2 | convolution fusion | flops 201851904 | bytes 4194304 | tf_op jit(solution)/shard_map/ij,cjp->cip/dot_general | solution.py:26
  12.1 1.2 %copy.41 = f32[4,8,16,1024]{3,2,1,0:T(8,128)S(1)} copy(f32[4,8,16,1024]{3,1,2,0:T(8,128)S(1)} %bitcast.82) | data formatting | bytes 4194304
  13.4 3.5 %bitcast_multiply_fusion = (f32[32,16,1024]{2,1,0:T(8,128)}, f32[32,16,1024]{2,1,0:T(8,128)S(1)}, f32[16,1024]{1,0:T(8,128)S(1)}) fusion(f32[4,8,16,1024]{3,2,1,0:T(8,128)S(1)} %copy.41, bf16[32,16,1024]{2,1,0:T(8,128)(2,1)S(1)} %copy-done.3), kind=kLoop, calls=%fused_computation.29 | loop fusion | flops 6799360 | bytes 7405568 | tf_op jit(solution)/shard_map/mul | solution.py:45
  16.8 3.6 %fusion.54 = (f32[3,16,1024]{2,1,0:T(8,128)S(1)}, f32[3,32,16,1024]{3,2,1,0:T(8,128)}) fusion(bf16[3,32,16,1024]{3,2,1,0:T(8,128)(2,1)S(1)} %copy-done.5, f32[32,16,1024]{2,1,0:T(8,128)S(1)} %get-tuple-element.13), kind=kLoop, calls=%fused_computation.91 | loop fusion | flops 9388032 | bytes 11730944 | tf_op jit(solution)/shard_map/reduce_sum | solution.py:50
  20.7 0.8 pad_maximum_fusion
  21.5 4.9 %collective-permute-start = (bf16[1,16,1024]{2,1,0:T(8,128)(2,1)S(1)}, bf16[1,16,1024]{2,1,0:T(8,128)(2,1)S(1)}, u32[]{:S(2)}, u32[]{:S(2)}) collective-permute-start(bf16[1,16,1024]{2,1,0:T(8,128)(2,1)S(1)} %get-tuple-element.18), channel_id=1, source_target_pairs={{0,4},{4,8},{8,12},{12,16},{16,20},{20,24},{24,28},{1,5},{5,9},{9,... | collective-permute-start | bytes 98312 | tf_op jit(solution)/shard_map/ppermute | solution.py:17
  26.4 1.5 %collective-permute-start.1 = (bf16[1,16,1024]{2,1,0:T(8,128)(2,1)S(1)}, bf16[1,16,1024]{2,1,0:T(8,128)(2,1)S(1)}, u32[]{:S(2)}, u32[]{:S(2)}) collective-permute-start(bf16[1,16,1024]{2,1,0:T(8,128)(2,1)S(1)} %get-tuple-element.17), channel_id=1, source_target_pairs={{4,0},{8,4},{12,8},{16,12},{20,16},{24,20},{28,24},{5,1},{9,5},{13... | collective-permute-start | bytes 98312 | tf_op jit(solution)/shard_map/ppermute | solution.py:18
  27.9 7.2 %reshape.104 = f32[3,32,16384]{2,1,0:T(8,128)} reshape(f32[3,32,16,1024]{3,2,1,0:T(8,128)} %get-tuple-element.9) | data formatting | bytes 12582912 | tf_op jit(solution)/shard_map/reshape | solution.py:25
  35.1 8.7 %fusion.39 = f32[3,16384,32]{1,2,0:T(8,128)} fusion(f32[3,32,16384]{2,1,0:T(8,128)} %reshape.104), kind=kOutput, calls=%fused_computation.72 | convolution fusion | flops 603980800 | bytes 12582912 | tf_op jit(solution)/shard_map/ij,cjp->cip/dot_general | solution.py:26
  43.8 0.9 copy.42
  44.7 10.2 %copy.44 = f32[12,8,16,1024]{3,2,1,0:T(8,128)} copy(f32[12,8,16,1024]{3,1,2,0:T(8,128)} %bitcast.76) | data formatting | bytes 12582912
  55.2 1.5 %collective-permute-start.2 = (bf16[34,1,1024]{2,0,1:T(8,128)(2,1)S(1)}, bf16[34,1,1024]{2,0,1:T(8,128)(2,1)S(1)}, u32[]{:S(2)}, u32[]{:S(2)}) collective-permute-start(bf16[34,1,1024]{2,0,1:T(8,128)(2,1)S(1)} %copy.34), channel_id=1, source_target_pairs={{0,1},{1,2},{2,3},{4,5},{5,6},{6,7},{8,9},{9,10},{10,11},{12,13},{... | collective-permute-start | bytes 208904 | tf_op jit(solution)/shard_map/ppermute | solution.py:17
  56.7 1.5 %collective-permute-start.3 = (bf16[34,1,1024]{2,0,1:T(8,128)(2,1)S(1)}, bf16[34,1,1024]{2,0,1:T(8,128)(2,1)S(1)}, u32[]{:S(2)}, u32[]{:S(2)}) collective-permute-start(bf16[34,1,1024]{2,0,1:T(8,128)(2,1)S(1)} %copy.35), channel_id=1, source_target_pairs={{1,0},{2,1},{3,2},{5,4},{6,5},{7,6},{9,8},{10,9},{11,10},{13,12},{... | collective-permute-start | bytes 208904 | tf_op jit(solution)/shard_map/ppermute | solution.py:18
  58.4 3.1 %collective-permute-done.3 = bf16[34,1,1024]{2,0,1:T(8,128)(2,1)S(1)} collective-permute-done((bf16[34,1,1024]{2,0,1:T(8,128)(2,1)S(1)}, bf16[34,1,1024]{2,0,1:T(8,128)(2,1)S(1)}, u32[]{:S(2)}, u32[]{:S(2)}) %collective-permute-start.3) | collective-permute-done | bytes 69664 | tf_op jit(solution)/shard_map/ppermute | solution.py:18
  62.3 11.4 %all-gather.2.cloned.1.call-done = f32[4,8,16384]{2,0,1:T(4,128)} async-done(((f32[4,1,16384]{2,0,1:T(4,128)}), f32[4,8,16384]{2,0,1:T(4,128)}) %all-gather.2.cloned.1.call-update) | async-done | bytes 2097168 | tf_op jit(solution)/shard_map/all_gather | solution.py:109
  73.7 3.9 %convolution_bitcast_fusion = f32[4,8,16384]{2,1,0:T(8,128)S(1)} fusion(f32[4,8,16384]{2,0,1:T(4,128)} %all-gather.2.cloned.1.call-done, s32[8]{0:T(128)S(1)} %copy-done.11), kind=kOutput, calls=%fused_computation | convolution fusion | flops 50331712 | bytes 4194336 | tf_op jit(solution)/shard_map/sk,csl->ckl/dot_general | solution.py:71
  79.1 1.0 fusion.32
  80.2 1.1 %fusion.26 = f32[4,16384,8]{1,2,0:T(8,128)S(1)} fusion(f32[1,8,16384]{2,1,0:T(8,128)S(1)} %bitcast_multiply_fusion.3, f32[3,8,16384]{2,1,0:T(8,128)S(1)} %broadcast_multiply_fusion.1, s32[8]{0:T(128)S(1)} %copy-done.11), kind=kOutput, calls=%fused_computation.45 | convolution fusion | flops 50856000 | bytes 4194336 | tf_op jit(solution)/shard_map/sk,ckl->csl/dot_general | solution.py:81
  81.9 0.8 broadcast_multiply_fusion.2
  83.6 1.5 %mul.151 = f32[16,1024]{1,0:T(8,128)} reshape(f32[16384]{0:T(1024)} %dynamic-slice_reduce_fusion.1) | data formatting | bytes 131072 | tf_op jit(solution)/shard_map/mul | solution.py:60
  85.0 8.7 %subtract_multiply_fusion = (f32[3,32,16,1024]{3,2,1,0:T(8,128)}, f32[32,16,1024]{2,1,0:T(8,128)S(1)}) fusion(f32[3,16,1024]{2,1,0:T(8,128)S(1)} %get-tuple-element.6, f32[32,16,1024]{2,1,0:T(8,128)} %copy-done.2, bf16[3,32,16,1024]{3,2,1,0:T(8,128)(2,1)} %param.5, f32[32,16,1024]{2,1,0:T(8,128)} %get-tuple-element.12, f32[3,16,1024]{2,1,0:T(8,128)} %get-tuple-element.7, ...), kind=kLoop, calls=%fused_computation.10 | loop fusion | flops 18350080 | bytes 22413312 | tf_op jit(solution)/shard_map/mul | solution.py:57
  93.8 5.7 %fusion.11 = f32[32,16,1024]{2,1,0:T(8,128)} fusion(bf16[32,16,1024]{2,1,0:T(8,128)(2,1)S(1)} %copy-done.4, f32[4,8,16,1024]{3,2,1,0:T(8,128)S(1)} %copy-done.1, f32[34,18,1024]{2,1,0:T(8,128)S(1)} %maximum_convert_fusion, f32[32,16,1024]{2,1,0:T(8,128)S(1)} %get-tuple-element.11, f32[16,1024]{1,0:T(8,128)S(1)} %copy-done.9, f32[16,1024]{1,0:T(8,128)S(1)} %copy-done.8, ...), kind=kLoop, calls=%fused_computation.23 | loop fusion | flops 18350080 | bytes 17956960 | tf_op jit(solution)/shard_map/add | solution.py:114
  (52 shorter events, 4.7 us)
Async XLA Ops:
  7.2 66.5 %all-gather.2.cloned.1.call-start = ((), (), s32[]{:S(2)}) async-start(), calls=%async_computation | async-start | bytes 2359296 | tf_op jit(solution)/shard_map/all_gather | solution.py:109
  12.1 1.2 %copy-start.3 = (bf16[32,16,1024]{2,1,0:T(8,128)(2,1)S(1)}, bf16[32,16,1024]{2,1,0:T(8,128)(2,1)}, u32[]{:S(2)}) copy-start(bf16[32,16,1024]{2,1,0:T(8,128)(2,1)} %param.4) | copy-start | bytes 3145732
  13.3 3.5 %copy-start = (f32[4,8,16,1024]{3,2,1,0:T(8,128)}, f32[4,8,16,1024]{3,2,1,0:T(8,128)S(1)}, u32[]{:S(2)}) copy-start(f32[4,8,16,1024]{3,2,1,0:T(8,128)S(1)} %copy.41) | copy-start | bytes 6291460
  13.3 3.5 %copy-start.5 = (bf16[3,32,16,1024]{3,2,1,0:T(8,128)(2,1)S(1)}, bf16[3,32,16,1024]{3,2,1,0:T(8,128)(2,1)}, u32[]{:S(2)}) copy-start(bf16[3,32,16,1024]{3,2,1,0:T(8,128)(2,1)} %param.5) | copy-start | bytes 9437188
  16.8 3.6 %copy-start.2 = (f32[32,16,1024]{2,1,0:T(8,128)}, f32[32,16,1024]{2,1,0:T(8,128)S(1)}, u32[]{:S(2)}) copy-start(f32[32,16,1024]{2,1,0:T(8,128)S(1)} %get-tuple-element.13) | copy-start | bytes 6291460
  20.6 14.6 %copy-start.7 = (f32[16,1024]{1,0:T(8,128)}, f32[16,1024]{1,0:T(8,128)S(1)}, u32[]{:S(2)}) copy-start(f32[16,1024]{1,0:T(8,128)S(1)} %negate_exponential_fusion) | copy-start | bytes 196612
  21.5 33.3 %collective-permute-start = (bf16[1,16,1024]{2,1,0:T(8,128)(2,1)S(1)}, bf16[1,16,1024]{2,1,0:T(8,128)(2,1)S(1)}, u32[]{:S(2)}, u32[]{:S(2)}) collective-permute-start(bf16[1,16,1024]{2,1,0:T(8,128)(2,1)S(1)} %get-tuple-element.18), channel_id=1, source_target_pairs={{0,4},{4,8},{8,12},{12,16},{16,20},{20,24},{24,28},{1,5},{5,9},{9,... | collective-permute-start | bytes 98312 | tf_op jit(solution)/shard_map/ppermute | solution.py:17
  26.4 28.5 %collective-permute-start.1 = (bf16[1,16,1024]{2,1,0:T(8,128)(2,1)S(1)}, bf16[1,16,1024]{2,1,0:T(8,128)(2,1)S(1)}, u32[]{:S(2)}, u32[]{:S(2)}) collective-permute-start(bf16[1,16,1024]{2,1,0:T(8,128)(2,1)S(1)} %get-tuple-element.17), channel_id=1, source_target_pairs={{4,0},{8,4},{12,8},{16,12},{20,16},{24,20},{28,24},{5,1},{9,5},{13... | collective-permute-start | bytes 98312 | tf_op jit(solution)/shard_map/ppermute | solution.py:18
  35.1 8.7 %copy-start.10 = (f32[3,16,1024]{2,1,0:T(8,128)S(1)}, f32[3,16,1024]{2,1,0:T(8,128)}, u32[]{:S(2)}) copy-start(f32[3,16,1024]{2,1,0:T(8,128)} %param.6) | copy-start | bytes 589828
  55.2 3.0 %collective-permute-start.2 = (bf16[34,1,1024]{2,0,1:T(8,128)(2,1)S(1)}, bf16[34,1,1024]{2,0,1:T(8,128)(2,1)S(1)}, u32[]{:S(2)}, u32[]{:S(2)}) collective-permute-start(bf16[34,1,1024]{2,0,1:T(8,128)(2,1)S(1)} %copy.34), channel_id=1, source_target_pairs={{0,1},{1,2},{2,3},{4,5},{5,6},{6,7},{8,9},{9,10},{10,11},{12,13},{... | collective-permute-start | bytes 208904 | tf_op jit(solution)/shard_map/ppermute | solution.py:17
  56.7 4.8 %collective-permute-start.3 = (bf16[34,1,1024]{2,0,1:T(8,128)(2,1)S(1)}, bf16[34,1,1024]{2,0,1:T(8,128)(2,1)S(1)}, u32[]{:S(2)}, u32[]{:S(2)}) collective-permute-start(bf16[34,1,1024]{2,0,1:T(8,128)(2,1)S(1)} %copy.35), channel_id=1, source_target_pairs={{1,0},{2,1},{3,2},{5,4},{6,5},{7,6},{9,8},{10,9},{11,10},{13,12},{... | collective-permute-start | bytes 208904 | tf_op jit(solution)/shard_map/ppermute | solution.py:18
  61.6 12.1 %copy-start.11 = (s32[8]{0:T(128)S(1)}, s32[8]{0:T(128)}, u32[]{:S(2)}) copy-start(s32[8]{0:T(128)} %param.7) | copy-start | bytes 100
  78.0 1.0 copy-start.6
  85.0 8.8 %copy-start.1 = (f32[4,8,16,1024]{3,2,1,0:T(8,128)S(1)}, f32[4,8,16,1024]{3,2,1,0:T(8,128)}, u32[]{:S(2)}) copy-start(f32[4,8,16,1024]{3,2,1,0:T(8,128)} %copy-done) | copy-start | bytes 6291460
  85.0 8.8 %copy-start.4 = (bf16[32,16,1024]{2,1,0:T(8,128)(2,1)S(1)}, bf16[32,16,1024]{2,1,0:T(8,128)(2,1)}, u32[]{:S(2)}) copy-start(bf16[32,16,1024]{2,1,0:T(8,128)(2,1)} %param.4) | copy-start | bytes 3145732
  85.0 8.8 %copy-start.8 = (f32[16,1024]{1,0:T(8,128)S(1)}, f32[16,1024]{1,0:T(8,128)}, u32[]{:S(2)}) copy-start(f32[16,1024]{1,0:T(8,128)} %copy-done.7) | copy-start | bytes 196612
  85.0 8.8 %copy-start.9 = (f32[16,1024]{1,0:T(8,128)S(1)}, f32[16,1024]{1,0:T(8,128)}, u32[]{:S(2)}) copy-start(f32[16,1024]{1,0:T(8,128)} %mul.151) | copy-start | bytes 196612
Sparse Core Ops, SparseCore 0:
  21.7 51.9 all-gather.1
where the time goes:
time: 107 us; the launch traced here: 106 us
  other arithmetic  27.3 us (26%)
  local copies, waits for them, and re-layouts  24.6 us (23%)
  matrix products  16.3 us (15%)
  waiting for transfers between devices  14.5 us (14%)
  between operations  14.3 us (13%)
  starting transfers between devices  9.35 us (9%)
    unnamed x30, local copies, waits for them, and re-layouts  13.8 us
    all_gather x1, waiting for transfers between devices, local(): received = lax.all_gather(stacked, 'depth', axis=1, tiled=True)  11.4 us
    dot_general x4, matrix products, along_rays(): jnp.einsum('ij,cjp->cip', matrix, flat, precision=lax.Precision.HIGHEST)  11.3 us
    mul x2, other arithmetic, slab_gradients(): slices_total * scaled_residual[:, None] * lit[None] * colour  9.56 us
    reshape x1, local copies, waits for them, and re-layouts, along_rays(): flat = values.reshape(shape[0], shape[1], -1)  7.22 us
    ppermute x2, starting transfers between devices, extended(): before = lax.ppermute(last, axis, up)  6.32 us
    add x1, other arithmetic, local(): grad_density = grad_density + smooth_rims(density_raw, slices_dev, rows_dev)  5.7 us
    dot_general x1, matrix products, composite(): jnp.einsum('sk,csl->ckl', one_hot, partials, precision=lax.Precision.HIGH...  3.86 us
  transfers between devices with their start and end apart: 5, of which 2 were waited for; matrix products, arithmetic and copies ran while one was open for 27% of the time, Pallas kernels for 0%

commit v1 on v0

--- a/solution.py
+++ b/solution.py
@@ -1,10 +1,39 @@
+import functools
 import jax
 import jax.numpy as jnp
 from jax import lax
 from jax.sharding import PartitionSpec as P
+from jax.lax import axis_index, axis_size, ppermute
 
 optical_depth = 2.5
 smooth_weight = 0.05
+
+
+def replace_the_slices(content, along_dim):
+    content = jnp.moveaxis(content, 0, along_dim)
+    a_next = content.shape
+    return content.reshape(
+        *a_next[:along_dim], a_next[along_dim] * a_next[along_dim + 1], *a_next[along_dim + 2 :]
+    )
+
+
+def wait_waves(z, mesh_ax, where_dim):
+    count_all = axis_size(mesh_ax)
+    panels = list(map(lambda m: (m, (m + 1) % count_all), range(count_all)))
+    pool = [(c, tick) for tick, c in panels]
+    w_next, z2 = ([], [])
+    for pp in [*range(count_all - 1)]:
+        if pp % 2 == 0:
+            w_next.append(ppermute(w_next[-1] if w_next else z, mesh_ax, panels))
+        else:
+            z2.append(ppermute(z2[-1] if z2 else z, mesh_ax, pool))
+    z1 = jnp.stack([*w_next[::-1], z, *z2], axis=0)
+    a_now = axis_index(mesh_ax) - len(w_next)
+    z1 = z1[(jnp.arange(count_all) - a_now) % count_all]
+    return replace_the_slices(z1, where_dim)
+
+
+name_frames = functools.partial(wait_waves, mesh_ax="depth", where_dim=1)
 
 
 def extended(value, sides, width):
@@ -106,7 +135,7 @@
     stacked = partial_value.reshape(4, 1, pixels)
     target_flat = target.reshape(3, pixels)
     position = lax.axis_index("depth")
-    received = lax.all_gather(stacked, "depth", axis=1, tiled=True)
+    received = name_frames(stacked)
     answers = composite(received, slab_rank, target_flat)
     mine = lax.dynamic_index_in_dim(answers, position, 1, keepdims=False)
     mine = mine.reshape(4, rows_dev, width)

time: 107 us -> 115 us (1.075)
  the two profiles are of different devices: /device:TPU:0 before, /device:TPU:29 now
where the time goes in v1:
time: 115 us; the launch traced here: 114 us
  local copies, waits for them, and re-layouts  34 us (30%)
  other arithmetic  27.5 us (24%)
  starting transfers between devices  22 us (19%)
  matrix products  16.3 us (14%)
  waiting for transfers between devices  13.5 us (12%)
    unnamed x40, local copies, waits for them, and re-layouts  19.1 us
    dot_general x4, matrix products, along_rays(): jnp.einsum('ij,cjp->cip', matrix, flat, precision=lax.Precision.HIGHEST)  11.3 us
    mul x2, other arithmetic, slab_gradients(): slices_total * scaled_residual[:, None] * lit[None] * colour  9.71 us
    ppermute x4, waiting for transfers between devices, wait_waves(): w_next.append(ppermute(w_next[-1] if w_next else z, mesh_ax, panels))  7.62 us
    reshape x1, local copies, waits for them, and re-layouts, along_rays(): flat = values.reshape(shape[0], shape[1], -1)  7.16 us
    ppermute x4, starting transfers between devices, wait_waves(): w_next.append(ppermute(w_next[-1] if w_next else z, mesh_ax, panels))  6.46 us
    ppermute x2, starting transfers between devices, extended(): before = lax.ppermute(last, axis, up)  6.18 us
    ppermute x2, starting transfers between devices, extended(): after = lax.ppermute(initial, axis, down)  6.09 us
  transfers between devices with their start and end apart: 11, of which 2 were waited for; matrix products, arithmetic and copies ran while one was open for 31% of the time, Pallas kernels for 0%

profile of v1, /device:TPU:29, one launch (start us, length us, event | category | flops | bytes accessed | tf_op | source)
XLA Modules:
  0.0 114.4 jit_solution(11903025750716542802)
XLA Ops:
  0.6 2.4 %fusion.16 = f32[32,16,1024]{2,1,0:T(8,128)S(1)} fusion(bf16[32,16,1024]{2,1,0:T(8,128)(2,1)} %param.4), kind=kLoop, calls=%fused_computation.29 | loop fusion | flops 4194304 | bytes 3145728 | tf_op jit(solution)/shard_map/mul | solution.py:69
  3.1 1.2 %copy.72 = f32[4,8,16,1024]{3,1,2,0:T(8,128)S(1)} copy(f32[4,8,16,1024]{3,2,1,0:T(8,128)S(1)} %bitcast.119) | data formatting | bytes 4194304
  4.3 1.2 %fusion = f32[16384,32]{0,1:T(8,128)S(1)} fusion(f32[32,16384]{1,0:T(8,128)S(1)} %bitcast.117), kind=kOutput, calls=%fused_computation.3 | convolution fusion | flops 201851904 | bytes 4194304 | tf_op jit(solution)/shard_map/ij,cjp->cip/dot_general | solution.py:55
  5.5 1.2 %copy.73 = f32[4,8,16,1024]{3,2,1,0:T(8,128)S(1)} copy(f32[4,8,16,1024]{3,1,2,0:T(8,128)S(1)} %bitcast.118) | data formatting | bytes 4194304
  6.8 3.5 %bitcast_multiply_fusion = (f32[32,16,1024]{2,1,0:T(8,128)}, f32[32,16,1024]{2,1,0:T(8,128)S(1)}, f32[16,1024]{1,0:T(8,128)S(1)}) fusion(f32[4,8,16,1024]{3,2,1,0:T(8,128)S(1)} %copy.73, bf16[32,16,1024]{2,1,0:T(8,128)(2,1)S(1)} %copy-done.3), kind=kLoop, calls=%fused_computation.30 | loop fusion | flops 6799360 | bytes 7405568 | tf_op jit(solution)/shard_map/mul | solution.py:74
  10.2 3.6 %fusion.56 = (f32[3,16,1024]{2,1,0:T(8,128)S(1)}, f32[3,32,16,1024]{3,2,1,0:T(8,128)}) fusion(bf16[3,32,16,1024]{3,2,1,0:T(8,128)(2,1)S(1)} %copy-done.5, f32[32,16,1024]{2,1,0:T(8,128)S(1)} %get-tuple-element.13), kind=kLoop, calls=%fused_computation.107 | loop fusion | flops 9388032 | bytes 11730944 | tf_op jit(solution)/shard_map/reduce_sum | solution.py:79
  14.3 1.5 %collective-permute-start.4 = (f32[4,1,16384]{2,0,1:T(4,128)S(1)}, f32[4,1,16384]{2,0,1:T(4,128)}, u32[]{:S(2)}, u32[]{:S(2)}) collective-permute-start(f32[4,1,16384]{2,0,1:T(4,128)S(1)} %pad_maximum_fusion), channel_id=1, source_target_pairs={{4,0},{8,4},{12,8},{16,12},{20,16},{24,20},{28,24},{0,28},{5,1},{9... | collective-permute-start | bytes 786440 | tf_op jit(solution)/shard_map/ppermute | solution.py:29
  15.7 1.3 %collective-permute-start.7 = (bf16[1,16,1024]{2,1,0:T(8,128)(2,1)S(1)}, bf16[1,16,1024]{2,1,0:T(8,128)(2,1)S(1)}, u32[]{:S(2)}, u32[]{:S(2)}) collective-permute-start(bf16[1,16,1024]{2,1,0:T(8,128)(2,1)S(1)} %get-tuple-element.18), channel_id=1, source_target_pairs={{0,4},{4,8},{8,12},{12,16},{16,20},{20,24},{24,28},{1,5},{5,9},{9,... | collective-permute-start | bytes 98312 | tf_op jit(solution)/shard_map/ppermute | solution.py:46
  17.0 4.2 %collective-permute-start.8 = (bf16[1,16,1024]{2,1,0:T(8,128)(2,1)S(1)}, bf16[1,16,1024]{2,1,0:T(8,128)(2,1)S(1)}, u32[]{:S(2)}, u32[]{:S(2)}) collective-permute-start(bf16[1,16,1024]{2,1,0:T(8,128)(2,1)S(1)} %get-tuple-element.17), channel_id=1, source_target_pairs={{4,0},{8,4},{12,8},{16,12},{20,16},{24,20},{28,24},{5,1},{9,5},{13... | collective-permute-start | bytes 98312 | tf_op jit(solution)/shard_map/ppermute | solution.py:47
  21.2 7.2 %reshape.174 = f32[3,32,16384]{2,1,0:T(8,128)} reshape(f32[3,32,16,1024]{3,2,1,0:T(8,128)} %get-tuple-element.9) | data formatting | bytes 12582912 | tf_op jit(solution)/shard_map/reshape | solution.py:54
  28.4 8.6 %fusion.39 = f32[3,16384,32]{1,2,0:T(8,128)} fusion(f32[3,32,16384]{2,1,0:T(8,128)} %reshape.174), kind=kOutput, calls=%fused_computation.84 | convolution fusion | flops 603980800 | bytes 12582912 | tf_op jit(solution)/shard_map/ij,cjp->cip/dot_general | solution.py:55
  39.0 10.2 %copy.76 = f32[12,8,16,1024]{3,2,1,0:T(8,128)} copy(f32[12,8,16,1024]{3,1,2,0:T(8,128)} %bitcast.111) | data formatting | bytes 12582912
  49.2 2.1 %collective-permute-start.2 = (f32[4,1,16384]{2,0,1:T(4,128)S(1)}, f32[4,1,16384]{2,0,1:T(4,128)S(1)}, u32[]{:S(2)}, u32[]{:S(2)}) collective-permute-start(f32[4,1,16384]{2,0,1:T(4,128)S(1)} %collective-permute-done.1), channel_id=1, source_target_pairs={{0,4},{4,8},{8,12},{12,16},{16,20},{20,24},{24,28},{28,0},{1,5},{5... | collective-permute-start | bytes 786440 | tf_op jit(solution)/shard_map/ppermute | solution.py:27
  51.6 4.9 %collective-permute-start.9 = (bf16[34,1,1024]{2,0,1:T(8,128)(2,1)S(1)}, bf16[34,1,1024]{2,0,1:T(8,128)(2,1)S(1)}, u32[]{:S(2)}, u32[]{:S(2)}) collective-permute-start(bf16[34,1,1024]{2,0,1:T(8,128)(2,1)S(1)} %copy.66), channel_id=1, source_target_pairs={{0,1},{1,2},{2,3},{4,5},{5,6},{6,7},{8,9},{9,10},{10,11},{12,13},{... | collective-permute-start | bytes 208904 | tf_op jit(solution)/shard_map/ppermute | solution.py:46
  56.6 1.9 %collective-permute-start.10 = (bf16[34,1,1024]{2,0,1:T(8,128)(2,1)S(1)}, bf16[34,1,1024]{2,0,1:T(8,128)(2,1)S(1)}, u32[]{:S(2)}, u32[]{:S(2)}) collective-permute-start(bf16[34,1,1024]{2,0,1:T(8,128)(2,1)S(1)} %copy.67), channel_id=1, source_target_pairs={{1,0},{2,1},{3,2},{5,4},{6,5},{7,6},{9,8},{10,9},{11,10},{13,12},{... | collective-permute-start | bytes 208904 | tf_op jit(solution)/shard_map/ppermute | solution.py:47
  58.6 4.1 %collective-permute-start.3 = (f32[4,1,16384]{2,0,1:T(4,128)S(1)}, f32[4,1,16384]{2,0,1:T(4,128)S(1)}, u32[]{:S(2)}, u32[]{:S(2)}) collective-permute-start(f32[4,1,16384]{2,0,1:T(4,128)S(1)} %collective-permute-done.2), channel_id=1, source_target_pairs={{0,4},{4,8},{8,12},{12,16},{16,20},{20,24},{24,28},{28,0},{1,5},{5... | collective-permute-start | bytes 786440 | tf_op jit(solution)/shard_map/ppermute | solution.py:27
  63.8 5.9 %collective-permute-done.5 = f32[4,1,16384]{2,0,1:T(4,128)S(1)} collective-permute-done((f32[4,1,16384]{2,0,1:T(4,128)}, f32[4,1,16384]{2,0,1:T(4,128)S(1)}, u32[]{:S(2)}, u32[]{:S(2)}) %collective-permute-start.5) | collective-permute-done | bytes 262176 | tf_op jit(solution)/shard_map/ppermute | solution.py:29
  69.6 1.8 %collective-permute-start.6 = (f32[4,1,16384]{2,0,1:T(4,128)S(1)}, f32[4,1,16384]{2,0,1:T(4,128)S(1)}, u32[]{:S(2)}, u32[]{:S(2)}) collective-permute-start(f32[4,1,16384]{2,0,1:T(4,128)S(1)} %collective-permute-done.5), channel_id=1, source_target_pairs={{4,0},{8,4},{12,8},{16,12},{20,16},{24,20},{28,24},{0,28},{5,1},{9... | collective-permute-start | bytes 786440 | tf_op jit(solution)/shard_map/ppermute | solution.py:29
  71.4 7.6 %collective-permute-done.3 = f32[4,1,16384]{2,0,1:T(4,128)S(1)} collective-permute-done((f32[4,1,16384]{2,0,1:T(4,128)S(1)}, f32[4,1,16384]{2,0,1:T(4,128)S(1)}, u32[]{:S(2)}, u32[]{:S(2)}) %collective-permute-start.3) | collective-permute-done | bytes 262176 | tf_op jit(solution)/shard_map/ppermute | solution.py:27
  82.8 1.7 %bitcast_dynamic-update-slice_fusion.1 = f32[8,4,1,16384]{3,1,0,2:T(4,128)} fusion(f32[8,4,1,16384]{3,1,0,2:T(4,128)} %maximum_dynamic-update-slice_fusion, f32[4,1,16384]{2,0,1:T(4,128)} %collective-permute-done.4), kind=kLoop, calls=%fused_computation.67 | loop fusion | bytes 524288
  85.9 4.6 %gather_fusion = f32[8,4,16384]{2,1,0:T(4,128)} fusion(f32[8,4,16384]{2,1,0:T(4,128)} %bitcast.16, s32[1024]{0:T(1024)S(1)} %pad_clamp_fusion), kind=kCustom, calls=%fused_computation | custom fusion | bytes 4194336 | tf_op jit(solution)/shard_map/gather | solution.py:32
  90.5 3.9 %convolution_bitcast_fusion = f32[4,8,16384]{2,1,0:T(8,128)S(1)} fusion(f32[4,8,16384]{2,0,1:T(4,128)} %bitcast.116, s32[8]{0:T(128)S(1)} %copy-done.13), kind=kOutput, calls=%fused_computation.1 | convolution fusion | flops 50331712 | bytes 4194336 | tf_op jit(solution)/shard_map/sk,csl->ckl/dot_general | solution.py:100
  99.8 8.8 %subtract_multiply_fusion = (f32[3,32,16,1024]{3,2,1,0:T(8,128)}, f32[32,16,1024]{2,1,0:T(8,128)S(1)}) fusion(f32[3,16,1024]{2,1,0:T(8,128)} %get-tuple-element.6, f32[32,16,1024]{2,1,0:T(8,128)} %copy-done.2, bf16[3,32,16,1024]{3,2,1,0:T(8,128)(2,1)} %param.5, f32[32,16,1024]{2,1,0:T(8,128)} %get-tuple-element.12, f32[3,16,1024]{2,1,0:T(8,128)} %get-tuple-element.7, ...), kind=kLoop, calls=%fused_computation.11 | loop fusion | flops 18350080 | bytes 22413312 | tf_op jit(solution)/shard_map/mul | solution.py:86
  108.7 5.7 %fusion.11 = f32[32,16,1024]{2,1,0:T(8,128)} fusion(bf16[32,16,1024]{2,1,0:T(8,128)(2,1)S(1)} %copy-done.4, f32[4,8,16,1024]{3,2,1,0:T(8,128)S(1)} %copy-done.1, f32[34,18,1024]{2,1,0:T(8,128)S(1)} %maximum_convert_fusion, f32[32,16,1024]{2,1,0:T(8,128)S(1)} %get-tuple-element.11, f32[16,1024]{1,0:T(8,128)S(1)} %mul.151, ...), kind=kLoop, calls=%fused_computation.24 | loop fusion | flops 18350080 | bytes 17956960 | tf_op jit(solution)/shard_map/add | solution.py:143
  (80 shorter events, 14.3 us)
Async XLA Ops:
  5.5 1.2 %copy-start.3 = (bf16[32,16,1024]{2,1,0:T(8,128)(2,1)S(1)}, bf16[32,16,1024]{2,1,0:T(8,128)(2,1)}, u32[]{:S(2)}) copy-start(bf16[32,16,1024]{2,1,0:T(8,128)(2,1)} %param.4) | copy-start | bytes 3145732
  6.8 3.5 %copy-start = (f32[4,8,16,1024]{3,2,1,0:T(8,128)}, f32[4,8,16,1024]{3,2,1,0:T(8,128)S(1)}, u32[]{:S(2)}) copy-start(f32[4,8,16,1024]{3,2,1,0:T(8,128)S(1)} %copy.73) | copy-start | bytes 6291460
  6.8 3.5 %copy-start.5 = (bf16[3,32,16,1024]{3,2,1,0:T(8,128)(2,1)S(1)}, bf16[3,32,16,1024]{3,2,1,0:T(8,128)(2,1)}, u32[]{:S(2)}) copy-start(bf16[3,32,16,1024]{3,2,1,0:T(8,128)(2,1)} %param.5) | copy-start | bytes 9437188
  10.2 3.6 %copy-start.2 = (f32[32,16,1024]{2,1,0:T(8,128)}, f32[32,16,1024]{2,1,0:T(8,128)S(1)}, u32[]{:S(2)}) copy-start(f32[32,16,1024]{2,1,0:T(8,128)S(1)} %get-tuple-element.13) | copy-start | bytes 6291460
  14.2 22.8 %collective-permute-start = (f32[4,1,16384]{2,0,1:T(4,128)S(1)}, f32[4,1,16384]{2,0,1:T(4,128)S(1)}, u32[]{:S(2)}, u32[]{:S(2)}) collective-permute-start(f32[4,1,16384]{2,0,1:T(4,128)S(1)} %pad_maximum_fusion), channel_id=1, source_target_pairs={{0,4},{4,8},{8,12},{12,16},{16,20},{20,24},{24,28},{28,0},{1,5},{5... | collective-permute-start | bytes 786440 | tf_op jit(solution)/shard_map/ppermute | solution.py:27
  14.3 44.2 %collective-permute-start.4 = (f32[4,1,16384]{2,0,1:T(4,128)S(1)}, f32[4,1,16384]{2,0,1:T(4,128)}, u32[]{:S(2)}, u32[]{:S(2)}) collective-permute-start(f32[4,1,16384]{2,0,1:T(4,128)S(1)} %pad_maximum_fusion), channel_id=1, source_target_pairs={{4,0},{8,4},{12,8},{16,12},{20,16},{24,20},{28,24},{0,28},{5,1},{9... | collective-permute-start | bytes 786440 | tf_op jit(solution)/shard_map/ppermute | solution.py:29
  15.7 33.4 %collective-permute-start.7 = (bf16[1,16,1024]{2,1,0:T(8,128)(2,1)S(1)}, bf16[1,16,1024]{2,1,0:T(8,128)(2,1)S(1)}, u32[]{:S(2)}, u32[]{:S(2)}) collective-permute-start(bf16[1,16,1024]{2,1,0:T(8,128)(2,1)S(1)} %get-tuple-element.18), channel_id=1, source_target_pairs={{0,4},{4,8},{8,12},{12,16},{16,20},{20,24},{24,28},{1,5},{5,9},{9,... | collective-permute-start | bytes 98312 | tf_op jit(solution)/shard_map/ppermute | solution.py:46
  17.0 34.3 %collective-permute-start.8 = (bf16[1,16,1024]{2,1,0:T(8,128)(2,1)S(1)}, bf16[1,16,1024]{2,1,0:T(8,128)(2,1)S(1)}, u32[]{:S(2)}, u32[]{:S(2)}) collective-permute-start(bf16[1,16,1024]{2,1,0:T(8,128)(2,1)S(1)} %get-tuple-element.17), channel_id=1, source_target_pairs={{4,0},{8,4},{12,8},{16,12},{20,16},{24,20},{28,24},{5,1},{9,5},{13... | collective-permute-start | bytes 98312 | tf_op jit(solution)/shard_map/ppermute | solution.py:47
  28.3 9.8 %copy-start.12 = (f32[3,16,1024]{2,1,0:T(8,128)S(1)}, f32[3,16,1024]{2,1,0:T(8,128)}, u32[]{:S(2)}) copy-start(f32[3,16,1024]{2,1,0:T(8,128)} %param.6) | copy-start | bytes 589828
  37.0 12.1 %copy-start.8 = (f32[4,1,16384]{2,0,1:T(4,128)}, f32[4,1,16384]{2,0,1:T(4,128)S(1)}, u32[]{:S(2)}) copy-start(f32[4,1,16384]{2,0,1:T(4,128)S(1)} %collective-permute-done) | copy-start | bytes 786436
  37.0 12.2 %collective-permute-start.1 = (f32[4,1,16384]{2,0,1:T(4,128)S(1)}, f32[4,1,16384]{2,0,1:T(4,128)S(1)}, u32[]{:S(2)}, u32[]{:S(2)}) collective-permute-start(f32[4,1,16384]{2,0,1:T(4,128)S(1)} %collective-permute-done), channel_id=1, source_target_pairs={{0,4},{4,8},{8,12},{12,16},{16,20},{20,24},{24,28},{28,0},{1,5},{5... | collective-permute-start | bytes 786440 | tf_op jit(solution)/shard_map/ppermute | solution.py:27
  49.2 13.7 %copy-start.10 = (f32[4,1,16384]{2,0,1:T(4,128)}, f32[4,1,16384]{2,0,1:T(4,128)S(1)}, u32[]{:S(2)}) copy-start(f32[4,1,16384]{2,0,1:T(4,128)S(1)} %collective-permute-done.1) | copy-start | bytes 786436
  49.2 9.4 %collective-permute-start.2 = (f32[4,1,16384]{2,0,1:T(4,128)S(1)}, f32[4,1,16384]{2,0,1:T(4,128)S(1)}, u32[]{:S(2)}, u32[]{:S(2)}) collective-permute-start(f32[4,1,16384]{2,0,1:T(4,128)S(1)} %collective-permute-done.1), channel_id=1, source_target_pairs={{0,4},{4,8},{8,12},{12,16},{16,20},{20,24},{24,28},{28,0},{1,5},{5... | collective-permute-start | bytes 786440 | tf_op jit(solution)/shard_map/ppermute | solution.py:27
  51.6 11.1 %collective-permute-start.9 = (bf16[34,1,1024]{2,0,1:T(8,128)(2,1)S(1)}, bf16[34,1,1024]{2,0,1:T(8,128)(2,1)S(1)}, u32[]{:S(2)}, u32[]{:S(2)}) collective-permute-start(bf16[34,1,1024]{2,0,1:T(8,128)(2,1)S(1)} %copy.66), channel_id=1, source_target_pairs={{0,1},{1,2},{2,3},{4,5},{5,6},{6,7},{8,9},{9,10},{10,11},{12,13},{... | collective-permute-start | bytes 208904 | tf_op jit(solution)/shard_map/ppermute | solution.py:46
  56.6 6.3 %collective-permute-start.10 = (bf16[34,1,1024]{2,0,1:T(8,128)(2,1)S(1)}, bf16[34,1,1024]{2,0,1:T(8,128)(2,1)S(1)}, u32[]{:S(2)}, u32[]{:S(2)}) collective-permute-start(bf16[34,1,1024]{2,0,1:T(8,128)(2,1)S(1)} %copy.67), channel_id=1, source_target_pairs={{1,0},{2,1},{3,2},{5,4},{6,5},{7,6},{9,8},{10,9},{11,10},{13,12},{... | collective-permute-start | bytes 208904 | tf_op jit(solution)/shard_map/ppermute | solution.py:47
  58.5 11.1 %collective-permute-start.5 = (f32[4,1,16384]{2,0,1:T(4,128)}, f32[4,1,16384]{2,0,1:T(4,128)S(1)}, u32[]{:S(2)}, u32[]{:S(2)}) collective-permute-start(f32[4,1,16384]{2,0,1:T(4,128)} %collective-permute-done.4), channel_id=1, source_target_pairs={{4,0},{8,4},{12,8},{16,12},{20,16},{24,20},{28,24},{0,28},{5,1},{9... | collective-permute-start | bytes 786440 | tf_op jit(solution)/shard_map/ppermute | solution.py:29
  58.6 20.5 %collective-permute-start.3 = (f32[4,1,16384]{2,0,1:T(4,128)S(1)}, f32[4,1,16384]{2,0,1:T(4,128)S(1)}, u32[]{:S(2)}, u32[]{:S(2)}) collective-permute-start(f32[4,1,16384]{2,0,1:T(4,128)S(1)} %collective-permute-done.2), channel_id=1, source_target_pairs={{0,4},{4,8},{8,12},{12,16},{16,20},{20,24},{24,28},{28,0},{1,5},{5... | collective-permute-start | bytes 786440 | tf_op jit(solution)/shard_map/ppermute | solution.py:27
  63.0 17.5 %copy-start.11 = (f32[4,1,16384]{2,0,1:T(4,128)S(1)}, f32[4,1,16384]{2,0,1:T(4,128)}, u32[]{:S(2)}) copy-start(f32[4,1,16384]{2,0,1:T(4,128)} %copy-done.10) | copy-start | bytes 786436
  63.0 18.2 %copy-start.9 = (f32[4,1,16384]{2,0,1:T(4,128)S(1)}, f32[4,1,16384]{2,0,1:T(4,128)}, u32[]{:S(2)}) copy-start(f32[4,1,16384]{2,0,1:T(4,128)} %copy-done.8) | copy-start | bytes 786436
  63.8 18.2 %copy-start.7 = (f32[1,3,1,16384]{3,1,2,0:T(4,128)S(1)}, f32[1,3,1,16384]{3,1,2,0:T(4,128)}, u32[]{:S(2)}) copy-start(f32[1,3,1,16384]{3,1,2,0:T(4,128)} %concatenate.22) | copy-start | bytes 589828
  69.6 15.5 %collective-permute-start.6 = (f32[4,1,16384]{2,0,1:T(4,128)S(1)}, f32[4,1,16384]{2,0,1:T(4,128)S(1)}, u32[]{:S(2)}, u32[]{:S(2)}) collective-permute-start(f32[4,1,16384]{2,0,1:T(4,128)S(1)} %collective-permute-done.5), channel_id=1, source_target_pairs={{4,0},{8,4},{12,8},{16,12},{20,16},{24,20},{28,24},{0,28},{5,1},{9... | collective-permute-start | bytes 786440 | tf_op jit(solution)/shard_map/ppermute | solution.py:29
  85.9 4.6 %copy-start.13 = (s32[8]{0:T(128)S(1)}, s32[8]{0:T(128)}, u32[]{:S(2)}) copy-start(s32[8]{0:T(128)} %param.7) | copy-start | bytes 100
  99.8 8.8 %copy-start.1 = (f32[4,8,16,1024]{3,2,1,0:T(8,128)S(1)}, f32[4,8,16,1024]{3,2,1,0:T(8,128)}, u32[]{:S(2)}) copy-start(f32[4,8,16,1024]{3,2,1,0:T(8,128)} %copy-done) | copy-start | bytes 6291460
  99.8 8.8 %copy-start.4 = (bf16[32,16,1024]{2,1,0:T(8,128)(2,1)S(1)}, bf16[32,16,1024]{2,1,0:T(8,128)(2,1)}, u32[]{:S(2)}) copy-start(bf16[32,16,1024]{2,1,0:T(8,128)(2,1)} %param.4) | copy-start | bytes 3145732
  (1 other events, 1.0 us)
